TPU v7x, 32 devices: a whole 2x2x4 slice. The times are simulated.
32 devices in a mesh: clips: 2 (over y), patch: 4 (over z), span: 2 (over x), chan: 2 (over core).
Axes of the slice: x: 2, y: 2, z: 4, core: 2. Of those that a mesh axis runs over, the one named last changes fastest.
Arguments:
- latent_tiles: bfloat16 [4, 256, 4, 384], P(('clips', 'span'), 'patch'), parts along dimension 0, may hold values from -12 to 12
- route: int32 [4, 256], P(('clips', 'span')), parts along dimension 0, may hold values from 0 to 255, as said below
- w_query: bfloat16 [384, 384], replicated, may hold values from -0.5 to 4.6
- w_keyval: bfloat16 [384, 768], replicated, may hold values from -0.5 to 4.6
- conv_weight: bfloat16 [3, 3, 3, 384, 384], P(None, None, None, None, 'chan'), may hold values from -0.0625 to 0.0625
Outputs:
- decoded: bfloat16 [8, 8, 64, 384], P(('clips', 'span'), 'patch', None, 'chan'), parts along dimension 0
There are 2 independent parts, one for each index of `clips`. A program takes and returns all parts, laid end to end along the dimension named above; an argument that names none is the same for every part. Nothing has to cross between parts.
Inputs may be any that keep to these rules, and one draw needn't show every extreme that they name: `route`: each span's row is a permutation of 0 .. 255. The 64 tiles of positions j * 64 to (j + 1) * 64 - 1 go to at most 32 per owner, and in every span some such group sends exactly 32 to one owner.
All inputs are finite; a program needn't handle non-finite values.
Results may differ from a plain program's by a relative error of at most 0.0065.
Values may be sent and summed in bfloat16 or wider, within the bound.
No kernel may reach another device: no remote copies, remote signals or barrier semaphores. Data moves between devices by JAX's collectives and lax.ppermute only.
A program may use at most 64 MiB of HBM per device.

v0:
```python
import math
import jax
import jax.numpy as jnp
from jax import lax
from jax.sharding import PartitionSpec as P

C = 384
W = 64
RD = 2
FD = 2
epsilon = 1e-06


def scaled_rms(values):
    wide = values.astype(jnp.float32)
    return wide / jnp.sqrt(jnp.mean(wide * wide, axis=-1, keepdims=True) + epsilon)


def attend(queries, key_rows, value_rows):
    scale = 1.0 / math.sqrt(queries.shape[-1])
    scores = (
        jnp.einsum("fqc,fkc->fqk", queries, key_rows, preferred_element_type=jnp.float32) * scale
    )
    largest = jnp.max(scores, axis=-1, keepdims=True)
    powers = jnp.exp(scores - largest)
    totals = jnp.sum(powers, axis=-1, keepdims=True)
    weights = powers.astype(jnp.bfloat16)
    summed = jnp.einsum("fqk,fkc->fqc", weights, value_rows, preferred_element_type=jnp.float32)
    return summed / totals


def spatial_conv(frames, kernel):
    return lax.conv_general_dilated(
        frames,
        kernel,
        (1, 1),
        ((0, 0), (1, 1)),
        dimension_numbers=("NHWC", "HWIO", "NHWC"),
        preferred_element_type=jnp.float32,
    )


def local(latent_tiles, route, w_query, w_keyval, conv_weight):
    patch_count = lax.axis_size("patch")
    patch_index = lax.axis_index("patch")
    chan_count = lax.axis_size("chan")
    chan_index = lax.axis_index("chan")
    span_count = lax.axis_size("span")
    table = route[0]
    block = latent_tiles.shape[1]
    share = block // chan_count
    own_share = lax.dynamic_slice_in_dim(latent_tiles, chan_index * share, share, 1)
    every_tile = lax.all_gather(own_share, ("patch", "chan"), axis=1, tiled=True)[0]
    tile_total = every_tile.shape[0]
    rows = patch_count * RD
    slots = jnp.arange(tile_total, dtype=jnp.int32)
    one_hot = (slots[:, None] == table[None, :]).astype(jnp.bfloat16)
    placed = jnp.dot(
        one_hot, every_tile.reshape(tile_total, -1), preferred_element_type=jnp.float32
    ).astype(jnp.bfloat16)
    placed = placed.reshape(patch_count, FD, RD, W, C)
    whole = placed.transpose(1, 0, 2, 3, 4).reshape(FD, rows, W, C)
    normed_all = scaled_rms(whole).astype(jnp.bfloat16)
    padded = jnp.pad(whole, ((0, 0), (1, 1), (0, 0), (0, 0)))
    features = lax.dynamic_slice_in_dim(padded, patch_index * RD, RD + 2, 1)
    normed = scaled_rms(features).astype(jnp.bfloat16)
    ext_cells = (RD + 2) * W
    queries = jnp.einsum(
        "fnc,cd->fnd", normed.reshape(FD, ext_cells, C), w_query, preferred_element_type=jnp.float32
    ).astype(jnp.bfloat16)
    keyvals = jnp.einsum(
        "fnc,cd->fnd",
        normed_all.reshape(FD, rows * W, C),
        w_keyval,
        preferred_element_type=jnp.float32,
    ).astype(jnp.bfloat16)
    attended = attend(queries, keyvals[..., :C], keyvals[..., C:])
    mixed = (features.astype(jnp.float32) + attended.reshape(FD, RD + 2, W, C)).astype(jnp.bfloat16)
    row_ids = patch_index * RD - 1 + jnp.arange(RD + 2)
    inside = ((row_ids >= 0) & (row_ids < rows))[None, :, None, None]
    activated = jnp.where(inside, jax.nn.silu(scaled_rms(mixed)), 0.0).astype(jnp.bfloat16)
    by_first = spatial_conv(activated, conv_weight[0])
    by_middle = spatial_conv(activated[1:], conv_weight[1])
    to_next = jnp.concatenate([by_first[:1] + by_middle, by_first[1:]]).astype(jnp.bfloat16)
    pairs = [(i, i + 1) for i in range(span_count - 1)]
    from_prev = lax.ppermute(to_next, "span", pairs)
    by_last = spatial_conv(activated, conv_weight[2])
    own_middle = spatial_conv(activated[:1], conv_weight[1])
    own_sum = jnp.concatenate([by_last[:1], own_middle + by_last[1:]])
    out_width = conv_weight.shape[-1]
    own_rows = mixed[:, 1 : RD + 1]
    own_channels = lax.dynamic_slice_in_dim(own_rows, chan_index * out_width, out_width, 3)
    return (own_channels.astype(jnp.float32) + own_sum + from_prev.astype(jnp.float32)).astype(
        jnp.bfloat16
    )


def solution(mesh):
    placed = (
        P(("clips", "span"), "patch", None, None),
        P(("clips", "span"), None),
        P(),
        P(),
        P(None, None, None, None, "chan"),
    )
    return jax.shard_map(
        local,
        mesh=mesh,
        in_specs=placed,
        out_specs=P(("clips", "span"), "patch", None, "chan"),
        check_vma=False,
    )
```

profile of v0, /device:TPU:0, one launch (start us, length us, event | category | flops | bytes accessed | tf_op | source)
XLA Modules:
  0.0 41.3 jit_solution(17983313363802852854)
XLA Ops:
  0.0 0.0 copy-start
  0.0 0.0 copy-start.2
  0.0 1.0 %constant_dynamic-slice_fusion = bf16[1,32,4,384]{3,2,0,1:T(4,128)(2,1)S(1)} fusion(bf16[1,64,4,384]{3,2,0,1:T(4,128)(2,1)} %bitcast.114, s32[]{:T(128)S(6)} %select_n.13), kind=kLoop, calls=%fused_computation.87 | loop fusion | bytes 196612 | tf_op jit(solution)/shard_map/dynamic_slice | solution.py:52
  1.0 17.2 %all_gather.3 = bf16[1,256,4,384]{3,2,0,1:T(4,128)(2,1)S(1)} all-gather(bf16[1,32,4,384]{3,2,0,1:T(4,128)(2,1)S(1)} %constant_dynamic-slice_fusion), channel_id=1, replica_groups=mesh['clips'=2,'patch'=4,'span'=2,'chan'=2] {'patch','chan'}, dimensions={1}, use_global_device_ids=true | all-gather | bytes 884736 | tf_op jit(solution)/shard_map/all_gather | solution.py:53
  18.2 0.1 copy.120
  18.4 0.0 copy-done.2
  18.4 0.4 convolution_convert_fusion
  18.7 0.5 %reshape.60 = bf16[4,2,2,64,384]{4,3,2,1,0:T(8,128)(2,1)S(1)} reshape(bf16[256,1536]{1,0:T(8,128)(2,1)S(1)} %convolution_convert_fusion) | data formatting | bytes 1572864 | tf_op jit(solution)/shard_map/reshape | solution.py:61
  19.2 0.2 multiply_reduce_fusion
  19.4 1.4 %fusion.72 = (bf16[4,2,2,64,384]{4,3,2,0,1:T(8,128)(2,1)S(1)}, f32[2,4,2,64,384]{4,3,2,1,0:T(8,128)}) fusion(bf16[4,2,2,64,384]{4,3,2,1,0:T(8,128)(2,1)S(1)} %reshape.60), kind=kLoop, calls=%fused_computation.94 | loop fusion | flops 393216 | bytes 3145728 | tf_op jit(solution)/shard_map/reshape | solution.py:61
  20.8 0.0 copy-start.1
  20.9 0.1 sqrt.29
  21.0 0.2 fusion.28
  21.1 0.2 fusion.29
  21.3 0.9 %copy-done.1 = f32[2,4,2,64,384]{4,3,2,1,0:T(8,128)S(1)} copy-done((f32[2,4,2,64,384]{4,3,2,1,0:T(8,128)S(1)}, f32[2,4,2,64,384]{4,3,2,1,0:T(8,128)}, u32[]{:S(2)}) %copy-start.1) | copy-done | bytes 1572888
  22.2 0.2 fusion
  22.5 0.0 copy-done
  22.5 0.0 copy-start.4
  22.5 2.1 %convolution_convert_fusion.1 = bf16[2,512,768]{2,1,0:T(8,128)(2,1)} fusion(bf16[2,512,384]{2,1,0:T(8,128)(2,1)S(1)} %fusion, bf16[384,768]{1,0:T(8,128)(2,1)S(1)} %copy-done), kind=kOutput, calls=%fused_computation.2 | convolution fusion | flops 604766208 | bytes 2949120 | tf_op jit(solution)/shard_map/fnc,cd->fnd/dot_general | solution.py:71
  24.6 0.0 copy-done.4
  24.6 1.9 %fusion.74 = (f32[2,256]{1,0:T(2,128)S(1)}, f32[2,256,512]{2,1,0:T(8,128)S(1)}) fusion(bf16[2,512,768]{2,1,0:T(8,128)(2,1)} %convolution_convert_fusion.1, bf16[2,256,384]{2,1,0:T(8,128)(2,1)S(1)} %bitcast.112, bf16[384,384]{1,0:T(8,128)(2,1)S(1)} %copy-done.4), kind=kOutput, calls=%fused_computation.96 | convolution fusion | flops 353041920 | bytes 2525184 | tf_op jit(solution)/shard_map/fqc,fkc->fqk/dot_general | solution.py:22
  26.5 0.3 fusion.25
  26.9 1.6 %convolution_divide_fusion = f32[2,256,384]{2,1,0:T(8,128)S(1)} fusion(bf16[2,512,768]{2,1,0:T(8,128)(2,1)} %convolution_convert_fusion.1, f32[2,256,512]{2,1,0:T(8,128)S(1)} %get-tuple-element.14, f32[2,256]{1,0:T(2,128)S(1)} %get-tuple-element.13, f32[2,256]{1,0:T(2,128)S(1)} %fusion.25), kind=kOutput, calls=%fused_computation.17 | convolution fusion | flops 202047488 | bytes 2625536 | tf_op jit(solution)/shard_map/fqk,fkc->fqc/dot_general | solution.py:28
  28.5 0.2 fusion.27
  28.8 0.0 copy-start.3
  28.8 0.3 fusion.81
  29.1 0.3 select_convert_fusion
  29.4 0.0 copy-start.5
  29.5 0.4 copy.116
  29.9 0.2 copy.118
  30.1 0.1 pad.11.clone
  30.2 0.7 %copy-done.3 = bf16[3,3,3,384,192]{3,4,2,1,0:T(8,128)(2,1)S(1)} copy-done((bf16[3,3,3,384,192]{3,4,2,1,0:T(8,128)(2,1)S(1)}, bf16[3,3,3,384,192]{3,4,2,1,0:T(8,128)(2,1)}, u32[]{:S(2)}) %copy-start.3) | copy-done | bytes 3981336
  30.9 0.0 copy-done.5
  30.9 0.6 %fusion.22 = f32[2,8,9,192]{3,1,2,0:T(8,128)S(1)} fusion(bf16[3,3,3,384,192]{3,4,2,1,0:T(8,128)(2,1)S(1)} %copy-done.3, bf16[4,1,7,2,384]{4,2,3,0,1:T(8,128)(2,1)S(1)} %slice.72, bf16[4,1,8,9,384]{4,2,3,0,1:T(8,128)(2,1)S(1)} %copy.105, pred[8,9]{0,1:T(8,128)(4,1)S(1)} %copy-done.5), kind=kOutput, calls=%fused_computation.27 | convolution fusion | flops 191941632 | bytes 1710080 | tf_op jit(solution)/shard_map/conv_general_dilated | solution.py:33
  31.5 0.0 copy-start.6
  31.5 0.1 copy.106
  31.6 0.3 pad.5.clone
  31.9 0.1 slice.62
  32.0 0.5 %fusion.34 = bf16[4,2,8,11,384]{4,1,3,2,0:T(2,128)(2,1)S(1)} fusion(bf16[4,2,7,2,384]{4,1,3,2,0:T(2,128)(2,1)S(1)} %slice.62, bf16[4,2,8,9,384]{4,1,3,2,0:T(2,128)(2,1)S(1)} %bitcast.101), kind=kLoop, calls=%fused_computation.43 | loop fusion | flops 1622016 | bytes 1069056 | tf_op jit(solution)/shard_map/conv_general_dilated | solution.py:33
  32.5 0.0 copy-done.6
  32.5 0.7 %fusion.77 = (bf16[2,16,9,192]{3,1,2,0:T(8,128)(2,1)S(1)}, f32[2,16,9,192]{3,1,2,0:T(8,128)S(1)}) fusion(bf16[3,3,3,384,192]{3,4,2,1,0:T(8,128)(2,1)S(1)} %copy-done.3, bf16[4,2,8,11,384]{4,1,3,2,0:T(2,128)(2,1)S(1)} %fusion.34, pred[16,9]{0,1:T(8,128)(4,1)S(1)} %copy-done.6), kind=kOutput, calls=%fused_computation.97 | convolution fusion | flops 382316544 | bytes 2201600 | tf_op jit(solution)/shard_map/conv_general_dilated | solution.py:33
  33.2 0.1 copy.108
  33.4 0.1 slice.74
  33.5 0.2 copy.101
  33.8 3.4 %collective-permute-start = (bf16[2,2,64,192]{3,2,1,0:T(8,128)(2,1)S(1)}, bf16[2,2,64,192]{3,2,1,0:T(8,128)(2,1)S(1)}, u32[]{:S(2)}, u32[]{:S(2)}) collective-permute-start(bf16[2,2,64,192]{3,2,1,0:T(8,128)(2,1)S(1)} %pad_maximum_fusion), channel_id=1, source_target_pairs={{0,2},{1,3},{4,6},{5,7},{8,10},{9,11},{12,14},{13,15},{16,18},{17,... | collective-permute-start | bytes 294920 | tf_op jit(solution)/shard_map/ppermute | solution.py:86
  37.3 0.7 %fusion.11 = f32[2,16,9,192]{3,1,2,0:T(8,128)S(1)} fusion(bf16[3,3,3,384,192]{3,4,2,1,0:T(8,128)(2,1)S(1)} %copy-done.3, bf16[4,2,8,11,384]{4,1,3,2,0:T(2,128)(2,1)S(1)} %fusion.34, pred[16,9]{0,1:T(8,128)(4,1)S(1)} %copy-done.6), kind=kOutput, calls=%fused_computation.22 | convolution fusion | flops 382261248 | bytes 2091008 | tf_op jit(solution)/shard_map/conv_general_dilated | solution.py:33
  38.0 0.2 copy.117
  38.1 0.1 pad.7.clone
  38.3 0.6 %fusion.19 = f32[2,8,9,192]{3,1,2,0:T(8,128)S(1)} fusion(bf16[3,3,3,384,192]{3,4,2,1,0:T(8,128)(2,1)S(1)} %copy-done.3, bf16[4,1,7,2,384]{4,2,3,0,1:T(8,128)(2,1)S(1)} %slice.66, bf16[4,1,8,9,384]{4,2,3,0,1:T(8,128)(2,1)S(1)} %copy.98, pred[8,9]{0,1:T(8,128)(4,1)S(1)} %copy-done.5), kind=kOutput, calls=%fused_computation.26 | convolution fusion | flops 191941632 | bytes 1710080 | tf_op jit(solution)/shard_map/conv_general_dilated | solution.py:33
  38.9 0.1 copy.99
  39.0 0.2 copy.94
  39.4 1.1 %collective-permute-done = bf16[2,2,64,192]{3,2,1,0:T(8,128)(2,1)S(1)} collective-permute-done((bf16[2,2,64,192]{3,2,1,0:T(8,128)(2,1)S(1)}, bf16[2,2,64,192]{3,2,1,0:T(8,128)(2,1)S(1)}, u32[]{:S(2)}, u32[]{:S(2)}) %collective-permute-start) | collective-permute-done | bytes 98336 | tf_op jit(solution)/shard_map/ppermute | solution.py:86
  40.5 0.8 %fusion.58 = bf16[2,2,64,192]{3,2,1,0:T(8,128)(2,1)} fusion(f32[1,2,64,192]{3,2,1,0:T(8,128)S(1)} %get-tuple-element.12, f32[1,2,64,192]{3,2,1,0:T(8,128)S(1)} %get-tuple-element.11, bf16[2,2,64,192]{3,2,1,0:T(8,128)(2,1)S(1)} %collective-permute-done, bf16[2,2,64,384]{3,2,1,0:T(8,128)(2,1)S(1)} %slice.61, s32[]{:T(128)S(6)} %select_n.15), kind=kLoop, calls=%fused_computation.65 | loop fusion | flops 294912 | bytes 491524 | tf_op jit(solution)/shard_map/convert_element_type | solution.py:93
  (22 shorter events, 0.4 us)
Async XLA Ops:
  0.0 22.5 %copy-start = (bf16[384,768]{1,0:T(8,128)(2,1)S(1)}, bf16[384,768]{1,0:T(8,128)(2,1)}, u32[]{:S(2)}) copy-start(bf16[384,768]{1,0:T(8,128)(2,1)} %param.8) | copy-start | bytes 1769476
  0.0 18.4 %copy-start.2 = (s32[1,256]{1,0:T(1,128)S(1)}, s32[1,256]{1,0:T(1,128)}, u32[]{:S(2)}) copy-start(s32[1,256]{1,0:T(1,128)} %param.6) | copy-start | bytes 3076
  20.8 1.4 %copy-start.1 = (f32[2,4,2,64,384]{4,3,2,1,0:T(8,128)S(1)}, f32[2,4,2,64,384]{4,3,2,1,0:T(8,128)}, u32[]{:S(2)}) copy-start(f32[2,4,2,64,384]{4,3,2,1,0:T(8,128)} %get-tuple-element.8) | copy-start | bytes 4718596
  22.5 2.1 %copy-start.4 = (bf16[384,384]{1,0:T(8,128)(2,1)S(1)}, bf16[384,384]{1,0:T(8,128)(2,1)}, u32[]{:S(2)}) copy-start(bf16[384,384]{1,0:T(8,128)(2,1)} %param.7) | copy-start | bytes 884740
  28.8 2.1 %copy-start.3 = (bf16[3,3,3,384,192]{3,4,2,1,0:T(8,128)(2,1)S(1)}, bf16[3,3,3,384,192]{3,4,2,1,0:T(8,128)(2,1)}, u32[]{:S(2)}) copy-start(bf16[3,3,3,384,192]{3,4,2,1,0:T(8,128)(2,1)} %param.9) | copy-start | bytes 11943940
  29.4 1.4 %copy-start.5 = (pred[8,9]{0,1:T(8,128)(4,1)S(1)}, pred[8,9]{0,1:T(8,128)(4,1)}, u32[]{:S(2)}) copy-start(pred[8,9]{0,1:T(8,128)(4,1)} %constant.70) | copy-start | bytes 220
  31.5 1.0 %copy-start.6 = (pred[16,9]{0,1:T(8,128)(4,1)S(1)}, pred[16,9]{0,1:T(8,128)(4,1)}, u32[]{:S(2)}) copy-start(pred[16,9]{0,1:T(8,128)(4,1)} %constant.69) | copy-start | bytes 436
  33.8 6.7 %collective-permute-start = (bf16[2,2,64,192]{3,2,1,0:T(8,128)(2,1)S(1)}, bf16[2,2,64,192]{3,2,1,0:T(8,128)(2,1)S(1)}, u32[]{:S(2)}, u32[]{:S(2)}) collective-permute-start(bf16[2,2,64,192]{3,2,1,0:T(8,128)(2,1)S(1)} %pad_maximum_fusion), channel_id=1, source_target_pairs={{0,2},{1,3},{4,6},{5,7},{8,10},{9,11},{12,14},{13,15},{16,18},{17,... | collective-permute-start | bytes 294920 | tf_op jit(solution)/shard_map/ppermute | solution.py:86
where the time goes:
time: 41.5 us; the launch traced here: 41.3 us
  blocking collectives  17.2 us (41%)
  matrix products  8.7 us (21%)
  local copies, waits for them, and re-layouts  5.65 us (14%)
  other arithmetic  4.7 us (11%)
  starting transfers between devices  3.41 us (8%)
  waiting for transfers between devices  1.14 us (3%)
  between operations  0.43 us (1%)
    all_gather x1, blocking collectives, local(): lax.all_gather(own_share, ('patch', 'chan'), axis=1, tiled=True)[0]  17.2 us
    ppermute x1, starting transfers between devices, local(): from_prev = lax.ppermute(to_next, 'span', pairs)  3.41 us
    conv_general_dilated x4, matrix products, spatial_conv(): lax.conv_general_dilated(frames, kernel, (1, 1), ((0, 0), (1, 1)), dimens...  2.61 us
    unnamed x21, local copies, waits for them, and re-layouts  2.5 us
    dot_general x1, matrix products, local(): jnp.einsum('fnc,cd->fnd', normed_all.reshape(FD, rows * W, C), w_keyval,...  2.13 us
    dot_general x1, matrix products, attend(): jnp.einsum('fqc,fkc->fqk', queries, key_rows, preferred_element_type=jnp....  1.93 us
    dot_general x1, matrix products, attend(): jnp.einsum('fqk,fkc->fqc', weights, value_rows, preferred_element_type=jn...  1.65 us
    reshape x1, other arithmetic, local(): placed = placed.reshape(patch_count, FD, RD, W, C)  1.39 us
  transfers between devices with their start and end apart: 1, of which 1 were waited for; matrix products, arithmetic and copies ran while one was open for 5% of the time, Pallas kernels for 0%

commit v1 on v0

--- a/solution.py
+++ b/solution.py
@@ -9,6 +9,28 @@
 RD = 2
 FD = 2
 epsilon = 1e-06
+
+
+def laid_out(blocks, dim):
+    shape = list(blocks.shape[1:])
+    shape[dim] *= blocks.shape[0]
+    return jnp.moveaxis(blocks, 0, dim).reshape(shape)
+
+
+def ring_gather(x, axis, dim):
+    length = lax.axis_size(axis)
+    pairs = [(i, (i + 1) % length) for i in range(length)]
+    back = [(b, a) for a, b in pairs]
+    lower, upper = ([], [])
+    for step in range(length - 1):
+        if step % 2 == 0:
+            lower.append(lax.ppermute(lower[-1] if lower else x, axis, pairs))
+        else:
+            upper.append(lax.ppermute(upper[-1] if upper else x, axis, back))
+    tiles = jnp.stack([*lower[::-1], x, *upper])
+    shift = lax.axis_index(axis) - len(lower)
+    tiles = tiles[(jnp.arange(length) - shift) % length]
+    return laid_out(tiles, dim)
 
 
 def scaled_rms(values):
@@ -50,7 +72,7 @@
     block = latent_tiles.shape[1]
     share = block // chan_count
     own_share = lax.dynamic_slice_in_dim(latent_tiles, chan_index * share, share, 1)
-    every_tile = lax.all_gather(own_share, ("patch", "chan"), axis=1, tiled=True)[0]
+    every_tile = ring_gather(own_share, ("patch", "chan"), 1)[0]
     tile_total = every_tile.shape[0]
     rows = patch_count * RD
     slots = jnp.arange(tile_total, dtype=jnp.int32)

time: 41.5 us -> 53.1 us (1.28)
  blocking collectives: 17.2 us -> 0 us
  waiting for transfers between devices: 1.14 us -> 15.1 us
  starting transfers between devices: 3.41 us -> 15.7 us
  local copies, waits for them, and re-layouts: 5.65 us -> 8 us
    all_gather x1 -> x0, blocking collectives: 17.2 us -> none  [local(): lax.all_gather(own_share, ('patch', 'chan'), axis=1, tiled=True)[0]]
    ppermute x0 -> x7, waiting for transfers between devices: none -> 12.7 us  [the longest x4 12.6 us: ring_gather(): lower.append(lax.ppermute(lower[-1] if lower else x, axis, pairs))]
    ppermute x0 -> x7, starting transfers between devices: none -> 11.8 us  [the longest x3 11.3 us: ring_gather(): upper.append(lax.ppermute(upper[-1] if upper else x, axis, back))]
    gather x0 -> x1, local copies, waits for them, and re-layouts: none -> 1.29 us  [ring_gather(): tiles = tiles[(jnp.arange(length) - shift) % length]]
    ppermute x1, waiting for transfers between devices: 1.14 us -> 2.43 us  [local(): from_prev = lax.ppermute(to_next, 'span', pairs)]
    unnamed x21 -> x28, local copies, waits for them, and re-layouts: 2.5 us -> 3.51 us
    ppermute x1, starting transfers between devices: 3.41 us -> 3.96 us  [local(): from_prev = lax.ppermute(to_next, 'span', pairs)]
  transfers between devices with their start and end apart: 1 -> 8, of which waited for: 1 -> 5; matrix products, arithmetic and copies ran while one was open for 5% -> 2% of each run, Pallas kernels for 0% -> 0%
where the time goes in v1:
time: 53.1 us; the launch traced here: 52.8 us
  starting transfers between devices  15.7 us (30%)
  waiting for transfers between devices  15.1 us (28%)
  matrix products  8.71 us (16%)
  local copies, waits for them, and re-layouts  8 us (15%)
  other arithmetic  4.75 us (9%)
    ppermute x4, waiting for transfers between devices, ring_gather(): lower.append(lax.ppermute(lower[-1] if lower else x, axis, pairs))  12.6 us
    ppermute x3, starting transfers between devices, ring_gather(): upper.append(lax.ppermute(upper[-1] if upper else x, axis, back))  11.3 us
    ppermute x1, starting transfers between devices, local(): from_prev = lax.ppermute(to_next, 'span', pairs)  3.96 us
    unnamed x28, local copies, waits for them, and re-layouts  3.51 us
    conv_general_dilated x4, matrix products, spatial_conv(): lax.conv_general_dilated(frames, kernel, (1, 1), ((0, 0), (1, 1)), dimens...  2.61 us
    ppermute x1, waiting for transfers between devices, local(): from_prev = lax.ppermute(to_next, 'span', pairs)  2.43 us
    dot_general x1, matrix products, local(): jnp.einsum('fnc,cd->fnd', normed_all.reshape(FD, rows * W, C), w_keyval,...  2.13 us
    dot_general x1, matrix products, attend(): jnp.einsum('fqc,fkc->fqk', queries, key_rows, preferred_element_type=jnp....  1.93 us
  transfers between devices with their start and end apart: 8, of which 5 were waited for; matrix products, arithmetic and copies ran while one was open for 2% of the time, Pallas kernels for 0%

profile of v1, /device:TPU:0, one launch (start us, length us, event | category | flops | bytes accessed | tf_op | source)
XLA Modules:
  0.0 52.8 jit_solution(6447855888058519807)
XLA Ops:
  0.0 0.0 copy-start
  0.0 1.0 %constant_dynamic-slice_fusion = bf16[1,32,4,384]{3,2,1,0:T(4,128)(2,1)S(1)} fusion(bf16[1,64,4,384]{3,2,1,0:T(4,128)(2,1)} %param.5, s32[]{:T(128)S(6)} %select_n.37), kind=kLoop, calls=%fused_computation.101 | loop fusion | bytes 196612 | tf_op jit(solution)/shard_map/dynamic_slice | solution.py:74
  1.0 0.5 collective-permute-start
  1.5 4.1 %collective-permute-start.4 = (bf16[1,32,4,384]{3,2,1,0:T(4,128)(2,1)S(1)}, bf16[1,32,4,384]{3,2,1,0:T(4,128)(2,1)S(1)}, u32[]{:S(2)}, u32[]{:S(2)}) collective-permute-start(bf16[1,32,4,384]{3,2,1,0:T(4,128)(2,1)S(1)} %constant_dynamic-slice_fusion), channel_id=1, source_target_pairs={{1,0},{4,1},{5,4},{8,5},{9,8},{12,9},{13,12},{0,13},{3,2},{6,3},{7... | collective-permute-start | bytes 294920 | tf_op jit(solution)/shard_map/ppermute | solution.py:29
  5.6 2.3 %collective-permute-done = bf16[1,32,4,384]{3,2,1,0:T(4,128)(2,1)S(1)} collective-permute-done((bf16[1,32,4,384]{3,2,1,0:T(4,128)(2,1)S(1)}, bf16[1,32,4,384]{3,2,1,0:T(4,128)(2,1)S(1)}, u32[]{:S(2)}, u32[]{:S(2)}) %collective-permute-start) | collective-permute-done | bytes 98336 | tf_op jit(solution)/shard_map/ppermute | solution.py:27
  7.9 0.0 collective-permute-start.1
  7.9 5.8 %collective-permute-done.1 = bf16[1,32,4,384]{3,2,1,0:T(4,128)(2,1)S(1)} collective-permute-done((bf16[1,32,4,384]{3,2,1,0:T(4,128)(2,1)S(1)}, bf16[1,32,4,384]{3,2,1,0:T(4,128)(2,1)S(1)}, u32[]{:S(2)}, u32[]{:S(2)}) %collective-permute-start.1) | collective-permute-done | bytes 98336 | tf_op jit(solution)/shard_map/ppermute | solution.py:27
  13.7 0.0 collective-permute-start.2
  13.7 0.0 collective-permute-done.4
  13.8 3.6 %collective-permute-start.5 = (bf16[1,32,4,384]{3,2,1,0:T(4,128)(2,1)S(1)}, bf16[1,32,4,384]{3,2,1,0:T(4,128)(2,1)S(1)}, u32[]{:S(2)}, u32[]{:S(2)}) collective-permute-start(bf16[1,32,4,384]{3,2,1,0:T(4,128)(2,1)S(1)} %collective-permute-done.4), channel_id=1, source_target_pairs={{1,0},{4,1},{5,4},{8,5},{9,8},{12,9},{13,12},{0,13},{3,2},{6,3},{7... | collective-permute-start | bytes 294920 | tf_op jit(solution)/shard_map/ppermute | solution.py:29
  17.3 2.3 %collective-permute-done.2 = bf16[1,32,4,384]{3,2,1,0:T(4,128)(2,1)S(1)} collective-permute-done((bf16[1,32,4,384]{3,2,1,0:T(4,128)(2,1)S(1)}, bf16[1,32,4,384]{3,2,1,0:T(4,128)(2,1)S(1)}, u32[]{:S(2)}, u32[]{:S(2)}) %collective-permute-start.2) | collective-permute-done | bytes 98336 | tf_op jit(solution)/shard_map/ppermute | solution.py:27
  19.6 0.0 collective-permute-start.3
  19.7 0.0 collective-permute-done.5
  19.7 3.6 %collective-permute-start.6 = (bf16[1,32,4,384]{3,2,1,0:T(4,128)(2,1)S(1)}, bf16[1,32,4,384]{3,2,1,0:T(4,128)(2,1)S(1)}, u32[]{:S(2)}, u32[]{:S(2)}) collective-permute-start(bf16[1,32,4,384]{3,2,1,0:T(4,128)(2,1)S(1)} %collective-permute-done.5), channel_id=1, source_target_pairs={{1,0},{4,1},{5,4},{8,5},{9,8},{12,9},{13,12},{0,13},{3,2},{6,3},{7... | collective-permute-start | bytes 294920 | tf_op jit(solution)/shard_map/ppermute | solution.py:29
  23.3 2.2 %collective-permute-done.3 = bf16[1,32,4,384]{3,2,1,0:T(4,128)(2,1)S(1)} collective-permute-done((bf16[1,32,4,384]{3,2,1,0:T(4,128)(2,1)S(1)}, bf16[1,32,4,384]{3,2,1,0:T(4,128)(2,1)S(1)}, u32[]{:S(2)}, u32[]{:S(2)}) %collective-permute-start.3) | collective-permute-done | bytes 98336 | tf_op jit(solution)/shard_map/ppermute | solution.py:27
  25.7 0.9 %bitcast_dynamic-update-slice_fusion.3 = bf16[8,1,32,4,384]{4,3,2,1,0:T(4,128)(2,1)S(1)} fusion(bf16[8,1,32,4,384]{4,3,2,1,0:T(4,128)(2,1)S(1)} %bitcast_dynamic-update-slice_fusion.4, bf16[1,64,4,384]{3,2,1,0:T(4,128)(2,1)} %param.5, s32[]{:T(128)S(6)} %select_n.37), kind=kLoop, calls=%fused_computation.85 | loop fusion | bytes 196612
  26.7 0.0 collective-permute-done.6
  26.8 0.0 copy-start.2
  26.8 1.3 %gather_fusion = bf16[8,32,4,384]{3,2,1,0:T(4,128)(2,1)S(1)} fusion(bf16[8,32,4,384]{3,2,1,0:T(4,128)(2,1)S(1)} %bitcast.122, s32[1024]{0:T(1024)S(1)} %pad_clamp_fusion), kind=kCustom, calls=%fused_computation | custom fusion | bytes 1572896 | tf_op jit(solution)/shard_map/gather | solution.py:32
  28.1 0.1 copy.117
  28.2 0.0 copy-done.2
  28.3 0.4 convolution_convert_fusion
  28.6 0.5 reshape.109
  29.1 0.2 multiply_reduce_fusion
  29.3 1.4 %fusion.74 = (bf16[4,2,2,64,384]{4,3,2,0,1:T(8,128)(2,1)S(1)}, f32[2,4,2,64,384]{4,3,2,1,0:T(8,128)}) fusion(bf16[4,2,2,64,384]{4,3,2,1,0:T(8,128)(2,1)S(1)} %reshape.109), kind=kLoop, calls=%fused_computation.110 | loop fusion | flops 393216 | bytes 3145728 | tf_op jit(solution)/shard_map/reshape | solution.py:83
  30.8 0.1 sqrt.29
  30.9 0.2 fusion.28
  31.0 0.2 fusion.29
  31.2 0.9 %copy-done.1 = f32[2,4,2,64,384]{4,3,2,1,0:T(8,128)S(1)} copy-done((f32[2,4,2,64,384]{4,3,2,1,0:T(8,128)S(1)}, f32[2,4,2,64,384]{4,3,2,1,0:T(8,128)}, u32[]{:S(2)}) %copy-start.1) | copy-done | bytes 1572888
  32.2 0.2 fusion
  32.4 0.0 copy-start.4
  32.4 2.1 %convolution_convert_fusion.1 = bf16[2,512,768]{2,1,0:T(8,128)(2,1)} fusion(bf16[2,512,384]{2,1,0:T(8,128)(2,1)S(1)} %fusion, bf16[384,768]{1,0:T(8,128)(2,1)S(1)} %copy-done), kind=kOutput, calls=%fused_computation.3 | convolution fusion | flops 604766208 | bytes 2949120 | tf_op jit(solution)/shard_map/fnc,cd->fnd/dot_general | solution.py:93
  34.5 1.9 %fusion.76 = (f32[2,256]{1,0:T(2,128)S(1)}, f32[2,256,512]{2,1,0:T(8,128)S(1)}) fusion(bf16[2,512,768]{2,1,0:T(8,128)(2,1)} %convolution_convert_fusion.1, bf16[2,256,384]{2,1,0:T(8,128)(2,1)S(1)} %bitcast.130, bf16[384,384]{1,0:T(8,128)(2,1)S(1)} %copy-done.4), kind=kOutput, calls=%fused_computation.112 | convolution fusion | flops 353041920 | bytes 2525184 | tf_op jit(solution)/shard_map/fqc,fkc->fqk/dot_general | solution.py:44
  36.5 0.3 fusion.25
  36.8 1.7 %convolution_divide_fusion = f32[2,256,384]{2,1,0:T(8,128)S(1)} fusion(bf16[2,512,768]{2,1,0:T(8,128)(2,1)} %convolution_convert_fusion.1, f32[2,256,512]{2,1,0:T(8,128)S(1)} %get-tuple-element.14, f32[2,256]{1,0:T(2,128)S(1)} %get-tuple-element.13, f32[2,256]{1,0:T(2,128)S(1)} %fusion.25), kind=kOutput, calls=%fused_computation.18 | convolution fusion | flops 202047488 | bytes 2625536 | tf_op jit(solution)/shard_map/fqk,fkc->fqc/dot_general | solution.py:50
  38.5 0.2 fusion.27
  38.7 0.0 copy-start.3
  38.7 0.3 fusion.83
  39.0 0.3 select_convert_fusion
  39.4 0.0 copy-start.6
  39.4 0.4 copy.113
  39.8 0.3 pad.5.clone
  40.1 0.1 slice.64
  40.2 0.5 fusion.34
  40.7 0.1 copy-done.3
  40.8 0.7 %fusion.11 = f32[2,16,9,192]{3,1,2,0:T(8,128)S(1)} fusion(bf16[3,3,3,384,192]{3,4,2,1,0:T(8,128)(2,1)S(1)} %copy-done.3, bf16[4,2,8,11,384]{4,1,3,2,0:T(2,128)(2,1)S(1)} %fusion.34, pred[16,9]{0,1:T(8,128)(4,1)S(1)} %copy-done.6), kind=kOutput, calls=%fused_computation.23 | convolution fusion | flops 382261248 | bytes 2091008 | tf_op jit(solution)/shard_map/conv_general_dilated | solution.py:55
  41.6 0.7 %fusion.79 = (bf16[2,16,9,192]{3,1,2,0:T(8,128)(2,1)S(1)}, f32[2,16,9,192]{3,1,2,0:T(8,128)S(1)}) fusion(bf16[3,3,3,384,192]{3,4,2,1,0:T(8,128)(2,1)S(1)} %copy-done.3, bf16[4,2,8,11,384]{4,1,3,2,0:T(2,128)(2,1)S(1)} %fusion.34, pred[16,9]{0,1:T(8,128)(4,1)S(1)} %copy-done.6), kind=kOutput, calls=%fused_computation.113 | convolution fusion | flops 382316544 | bytes 2201600 | tf_op jit(solution)/shard_map/conv_general_dilated | solution.py:55
  42.3 0.0 copy-start.5
  42.3 0.2 copy.115
  42.5 0.1 pad.11.clone
  42.7 0.3 copy-done.5
  43.0 0.6 %fusion.22 = f32[2,8,9,192]{3,1,2,0:T(8,128)S(1)} fusion(bf16[3,3,3,384,192]{3,4,2,1,0:T(8,128)(2,1)S(1)} %copy-done.3, bf16[4,1,7,2,384]{4,2,3,0,1:T(8,128)(2,1)S(1)} %slice.74, bf16[4,1,8,9,384]{4,2,3,0,1:T(8,128)(2,1)S(1)} %copy.102, pred[8,9]{0,1:T(8,128)(4,1)S(1)} %copy-done.5), kind=kOutput, calls=%fused_computation.28 | convolution fusion | flops 191941632 | bytes 1710080 | tf_op jit(solution)/shard_map/conv_general_dilated | solution.py:55
  43.6 0.1 copy.103
  43.7 0.2 copy.114
  43.8 0.1 pad.7.clone
  44.0 0.6 %fusion.19 = f32[2,8,9,192]{3,1,2,0:T(8,128)S(1)} fusion(bf16[3,3,3,384,192]{3,4,2,1,0:T(8,128)(2,1)S(1)} %copy-done.3, bf16[4,1,7,2,384]{4,2,3,0,1:T(8,128)(2,1)S(1)} %slice.68, bf16[4,1,8,9,384]{4,2,3,0,1:T(8,128)(2,1)S(1)} %copy.95, pred[8,9]{0,1:T(8,128)(4,1)S(1)} %copy-done.5), kind=kOutput, calls=%fused_computation.27 | convolution fusion | flops 191941632 | bytes 1710080 | tf_op jit(solution)/shard_map/conv_general_dilated | solution.py:55
  44.6 0.1 copy.96
  44.7 0.1 copy.105
  44.8 0.1 slice.76
  44.9 0.2 copy.91
  45.2 0.2 copy.98
  45.6 4.0 %collective-permute-start.7 = (bf16[2,2,64,192]{3,2,1,0:T(8,128)(2,1)S(1)}, bf16[2,2,64,192]{3,2,1,0:T(8,128)(2,1)S(1)}, u32[]{:S(2)}, u32[]{:S(2)}) collective-permute-start(bf16[2,2,64,192]{3,2,1,0:T(8,128)(2,1)S(1)} %pad_maximum_fusion), channel_id=1, source_target_pairs={{0,2},{1,3},{4,6},{5,7},{8,10},{9,11},{12,14},{13,15},{16,18},{17,... | collective-permute-start | bytes 294920 | tf_op jit(solution)/shard_map/ppermute | solution.py:108
  49.6 2.4 %collective-permute-done.7 = bf16[2,2,64,192]{3,2,1,0:T(8,128)(2,1)S(1)} collective-permute-done((bf16[2,2,64,192]{3,2,1,0:T(8,128)(2,1)S(1)}, bf16[2,2,64,192]{3,2,1,0:T(8,128)(2,1)S(1)}, u32[]{:S(2)}, u32[]{:S(2)}) %collective-permute-start.7) | collective-permute-done | bytes 98336 | tf_op jit(solution)/shard_map/ppermute | solution.py:108
  52.0 0.8 %fusion.58 = bf16[2,2,64,192]{3,2,1,0:T(8,128)(2,1)} fusion(f32[1,2,64,192]{3,2,1,0:T(8,128)S(1)} %get-tuple-element.12, f32[1,2,64,192]{3,2,1,0:T(8,128)S(1)} %get-tuple-element.11, bf16[2,2,64,192]{3,2,1,0:T(8,128)(2,1)S(1)} %collective-permute-done.7, bf16[2,2,64,384]{3,2,1,0:T(8,128)(2,1)S(1)} %slice.63, s32[]{:T(128)S(6)} %select_n.41), kind=kLoop, calls=%fused_computation.66 | loop fusion | flops 294912 | bytes 491524 | tf_op jit(solution)/shard_map/convert_element_type | solution.py:115
  (35 shorter events, 0.7 us)
Async XLA Ops:
  0.0 32.4 %copy-start = (bf16[384,768]{1,0:T(8,128)(2,1)S(1)}, bf16[384,768]{1,0:T(8,128)(2,1)}, u32[]{:S(2)}) copy-start(bf16[384,768]{1,0:T(8,128)(2,1)} %param.8) | copy-start | bytes 1769476
  1.0 6.9 %collective-permute-start = (bf16[1,32,4,384]{3,2,1,0:T(4,128)(2,1)S(1)}, bf16[1,32,4,384]{3,2,1,0:T(4,128)(2,1)S(1)}, u32[]{:S(2)}, u32[]{:S(2)}) collective-permute-start(bf16[1,32,4,384]{3,2,1,0:T(4,128)(2,1)S(1)} %constant_dynamic-slice_fusion), channel_id=1, source_target_pairs={{0,1},{1,4},{4,5},{5,8},{8,9},{9,12},{12,13},{13,0},{2,3},{3,6},{6... | collective-permute-start | bytes 294920 | tf_op jit(solution)/shard_map/ppermute | solution.py:27
  1.5 12.2 %collective-permute-start.4 = (bf16[1,32,4,384]{3,2,1,0:T(4,128)(2,1)S(1)}, bf16[1,32,4,384]{3,2,1,0:T(4,128)(2,1)S(1)}, u32[]{:S(2)}, u32[]{:S(2)}) collective-permute-start(bf16[1,32,4,384]{3,2,1,0:T(4,128)(2,1)S(1)} %constant_dynamic-slice_fusion), channel_id=1, source_target_pairs={{1,0},{4,1},{5,4},{8,5},{9,8},{12,9},{13,12},{0,13},{3,2},{6,3},{7... | collective-permute-start | bytes 294920 | tf_op jit(solution)/shard_map/ppermute | solution.py:29
  7.9 5.8 %collective-permute-start.1 = (bf16[1,32,4,384]{3,2,1,0:T(4,128)(2,1)S(1)}, bf16[1,32,4,384]{3,2,1,0:T(4,128)(2,1)S(1)}, u32[]{:S(2)}, u32[]{:S(2)}) collective-permute-start(bf16[1,32,4,384]{3,2,1,0:T(4,128)(2,1)S(1)} %collective-permute-done), channel_id=1, source_target_pairs={{0,1},{1,4},{4,5},{5,8},{8,9},{9,12},{12,13},{13,0},{2,3},{3,6},{6... | collective-permute-start | bytes 294920 | tf_op jit(solution)/shard_map/ppermute | solution.py:27
  13.7 5.9 %collective-permute-start.2 = (bf16[1,32,4,384]{3,2,1,0:T(4,128)(2,1)S(1)}, bf16[1,32,4,384]{3,2,1,0:T(4,128)(2,1)S(1)}, u32[]{:S(2)}, u32[]{:S(2)}) collective-permute-start(bf16[1,32,4,384]{3,2,1,0:T(4,128)(2,1)S(1)} %collective-permute-done.1), channel_id=1, source_target_pairs={{0,1},{1,4},{4,5},{5,8},{8,9},{9,12},{12,13},{13,0},{2,3},{3,6},{6... | collective-permute-start | bytes 294920 | tf_op jit(solution)/shard_map/ppermute | solution.py:27
  13.8 5.9 %collective-permute-start.5 = (bf16[1,32,4,384]{3,2,1,0:T(4,128)(2,1)S(1)}, bf16[1,32,4,384]{3,2,1,0:T(4,128)(2,1)S(1)}, u32[]{:S(2)}, u32[]{:S(2)}) collective-permute-start(bf16[1,32,4,384]{3,2,1,0:T(4,128)(2,1)S(1)} %collective-permute-done.4), channel_id=1, source_target_pairs={{1,0},{4,1},{5,4},{8,5},{9,8},{12,9},{13,12},{0,13},{3,2},{6,3},{7... | collective-permute-start | bytes 294920 | tf_op jit(solution)/shard_map/ppermute | solution.py:29
  19.6 5.8 %collective-permute-start.3 = (bf16[1,32,4,384]{3,2,1,0:T(4,128)(2,1)S(1)}, bf16[1,32,4,384]{3,2,1,0:T(4,128)(2,1)S(1)}, u32[]{:S(2)}, u32[]{:S(2)}) collective-permute-start(bf16[1,32,4,384]{3,2,1,0:T(4,128)(2,1)S(1)} %collective-permute-done.2), channel_id=1, source_target_pairs={{0,1},{1,4},{4,5},{5,8},{8,9},{9,12},{12,13},{13,0},{2,3},{3,6},{6... | collective-permute-start | bytes 294920 | tf_op jit(solution)/shard_map/ppermute | solution.py:27
  19.7 7.1 %collective-permute-start.6 = (bf16[1,32,4,384]{3,2,1,0:T(4,128)(2,1)S(1)}, bf16[1,32,4,384]{3,2,1,0:T(4,128)(2,1)S(1)}, u32[]{:S(2)}, u32[]{:S(2)}) collective-permute-start(bf16[1,32,4,384]{3,2,1,0:T(4,128)(2,1)S(1)} %collective-permute-done.5), channel_id=1, source_target_pairs={{1,0},{4,1},{5,4},{8,5},{9,8},{12,9},{13,12},{0,13},{3,2},{6,3},{7... | collective-permute-start | bytes 294920 | tf_op jit(solution)/shard_map/ppermute | solution.py:29
  26.8 1.4 %copy-start.2 = (s32[1,256]{1,0:T(1,128)S(1)}, s32[1,256]{1,0:T(1,128)}, u32[]{:S(2)}) copy-start(s32[1,256]{1,0:T(1,128)} %param.6) | copy-start | bytes 3076
  30.8 1.4 %copy-start.1 = (f32[2,4,2,64,384]{4,3,2,1,0:T(8,128)S(1)}, f32[2,4,2,64,384]{4,3,2,1,0:T(8,128)}, u32[]{:S(2)}) copy-start(f32[2,4,2,64,384]{4,3,2,1,0:T(8,128)} %get-tuple-element.8) | copy-start | bytes 4718596
  32.4 2.1 %copy-start.4 = (bf16[384,384]{1,0:T(8,128)(2,1)S(1)}, bf16[384,384]{1,0:T(8,128)(2,1)}, u32[]{:S(2)}) copy-start(bf16[384,384]{1,0:T(8,128)(2,1)} %param.7) | copy-start | bytes 884740
  38.7 2.1 %copy-start.3 = (bf16[3,3,3,384,192]{3,4,2,1,0:T(8,128)(2,1)S(1)}, bf16[3,3,3,384,192]{3,4,2,1,0:T(8,128)(2,1)}, u32[]{:S(2)}) copy-start(bf16[3,3,3,384,192]{3,4,2,1,0:T(8,128)(2,1)} %param.9) | copy-start | bytes 11943940
  39.4 1.4 %copy-start.6 = (pred[16,9]{0,1:T(8,128)(4,1)S(1)}, pred[16,9]{0,1:T(8,128)(4,1)}, u32[]{:S(2)}) copy-start(pred[16,9]{0,1:T(8,128)(4,1)} %constant.87) | copy-start | bytes 436
  42.3 0.7 %copy-start.5 = (pred[8,9]{0,1:T(8,128)(4,1)S(1)}, pred[8,9]{0,1:T(8,128)(4,1)}, u32[]{:S(2)}) copy-start(pred[8,9]{0,1:T(8,128)(4,1)} %constant.88) | copy-start | bytes 220
  45.6 6.5 %collective-permute-start.7 = (bf16[2,2,64,192]{3,2,1,0:T(8,128)(2,1)S(1)}, bf16[2,2,64,192]{3,2,1,0:T(8,128)(2,1)S(1)}, u32[]{:S(2)}, u32[]{:S(2)}) collective-permute-start(bf16[2,2,64,192]{3,2,1,0:T(8,128)(2,1)S(1)} %pad_maximum_fusion), channel_id=1, source_target_pairs={{0,2},{1,3},{4,6},{5,7},{8,10},{9,11},{12,14},{13,15},{16,18},{17,... | collective-permute-start | bytes 294920 | tf_op jit(solution)/shard_map/ppermute | solution.py:108
